TPU v7x, 128 devices: a whole 4x4x4 slice. The times are simulated.
128 devices in a mesh: outer: 16 (over z_hi, y, core), inner: 8 (over x, z_lo).
Axes of the slice: x: 4, y: 4, z: 4 (z_hi: 2, z_lo: 2; z = z_hi * 2 + z_lo), core: 2. Of those that a mesh axis runs over, the one named last changes fastest.
Arguments:
- q_load: bfloat16 [131072, 512], P(('outer', 'inner')), may hold values from -8 to 8
- kv_load: bfloat16 [131072, 256], P(('outer', 'inner')), may hold values from -8 to 8
- pack_dest: int32 [128, 8], P('outer'), may hold values from -1 to 31, as said below
- counts: int32 [128], P('outer'), may hold values from 0 to 8, as said below
- segment_ids: int32 [65536], P(('outer', 'inner')), may hold values from 0 to 7, never falling along the last dimension, each value on 1 to 16384 neighbouring positions
Outputs:
- attn_out: bfloat16 [65536, 512], P(('outer', 'inner'))
Inputs may be any that keep to these rules, and one draw needn't show every extreme that they name: In each group of 8 loader shards that share an outer index the counts add up to 32; some shard of every group holds 8 live blocks and some holds none. `pack_dest`: live entries of a group name every block number 0 to 31 exactly once; block number t goes to the device of inner index t // 4 in the same group, as its block t % 4; a shard sends at most 1 block to one device, and some shard sends exactly 1; entries of slots that are not live are -1. `segment_ids`: never falling along the sequence.
All inputs are finite; a program needn't handle non-finite values.
Results may differ from a plain program's by a relative error of at most 0.0059.
Values may be sent and summed in bfloat16 or wider, within the bound.
No kernel may reach another device: no remote copies, remote signals or barrier semaphores. Data moves between devices by JAX's collectives and lax.ppermute only.
A program may use at most 64 MiB of HBM per device.

v0:
```python
import math

import jax
import jax.numpy as jnp
from jax import lax
from jax.experimental import pallas as pl
from jax.experimental.pallas import tpu as pltpu
from jax.sharding import PartitionSpec as P


def shifted(value, axis, steps):
    count = lax.axis_size(axis)
    leading, last = (max(0, -steps), min(count, count - steps))
    return lax.ppermute(value, axis, [(source, source + steps) for source in range(leading, last)])


def select_rows(selector, blocks, pattern):
    return jnp.einsum(
        pattern, selector.astype(jnp.bfloat16), blocks, preferred_element_type=jnp.float32
    ).astype(jnp.bfloat16)


def local(q_load, kv_load, pack_dest, counts, segment_ids):
    group_width = lax.axis_size("inner")
    my_index = lax.axis_index("inner")
    capacity = pack_dest.shape[1]
    slot_count = capacity // 2
    pair_limit = -(-capacity // group_width)
    row_length = q_load.shape[0] // capacity
    query_width = q_load.shape[1]
    pair_width = kv_load.shape[1]
    head_size = pair_width // 2
    head_count = query_width // head_size
    slot_grid = lax.broadcasted_iota(jnp.int32, (group_width, capacity), 1)
    live_all = slot_grid < counts[:, None]
    owner_all = pack_dest // slot_count
    slot_numbers = jnp.arange(capacity, dtype=jnp.int32)
    earlier = slot_numbers[None, :] < slot_numbers[:, None]
    same_owner = owner_all[:, :, None] == owner_all[:, None, :]
    rank_all = jnp.sum(
        (earlier[None] & same_owner & live_all[:, None, :]).astype(jnp.int32), axis=2
    )
    shard_rows = jnp.arange(group_width, dtype=jnp.int32)
    mine_row = (shard_rows == my_index)[:, None]
    my_owner = jnp.sum(jnp.where(mine_row, owner_all, 0), axis=0)
    my_rank = jnp.sum(jnp.where(mine_row, rank_all, 0), axis=0)
    my_live = jnp.any(mine_row & live_all, axis=0)
    pair_ids = jnp.arange(pair_limit, dtype=jnp.int32)
    send_select = (
        my_live[None, None, :]
        & (my_owner[None, None, :] == shard_rows[:, None, None])
        & (my_rank[None, None, :] == pair_ids[None, :, None])
    )
    q_blocks = q_load.reshape(capacity, row_length, query_width)
    kv_blocks = kv_load.reshape(capacity, row_length, pair_width)
    send_q = select_rows(send_select, q_blocks, "jkc,crf->jkrf")
    send_kv = select_rows(send_select, kv_blocks, "jkc,crf->jkrf")
    recv_kv = lax.all_to_all(send_kv, "inner", split_axis=0, concat_axis=0, tiled=True)
    wanted = my_index * slot_count + jnp.arange(slot_count, dtype=jnp.int32)
    take_select = jnp.any(
        live_all[None, :, None, :]
        & (pack_dest[None, :, None, :] == wanted[:, None, None, None])
        & (rank_all[None, :, None, :] == pair_ids[None, None, :, None]),
        axis=3,
    )
    kv_seq = select_rows(take_select, recv_kv, "srk,rktf->stf").reshape(
        slot_count * row_length, pair_width
    )
    tok_rows = slot_count * row_length
    owner_index = lax.axis_index(("outer", "inner"))
    outer_index = lax.axis_index("outer")
    score_scale = 1.0 / math.sqrt(head_size)
    extra_rows = 16
    seg_rows = tok_rows // pair_width
    seg_pad = jnp.zeros((extra_rows - seg_rows, pair_width), jnp.bfloat16)
    packed = jnp.concatenate(
        [kv_seq, segment_ids.astype(jnp.bfloat16).reshape(seg_rows, pair_width), seg_pad], axis=0
    )
    outer_reach = -(-(lax.axis_size("outer") * group_width // 4) // group_width)
    own_steps = list(range(0, outer_reach + 1, 2))
    partner_steps = list(range(1, outer_reach + 1, 2))
    moved = [packed if step == 0 else shifted(packed, "outer", step) for step in own_steps]
    own_stack = jnp.stack(moved)
    pair_mate = lax.ppermute(own_stack, "inner", [(i, i ^ 1) for i in range(group_width)])
    pair = jnp.stack([own_stack, pair_mate])
    send_q = lax.optimization_barrier((send_q, pair_mate))[0]
    recv_q = lax.all_to_all(send_q, "inner", split_axis=0, concat_axis=0, tiled=True)
    q_seq = select_rows(take_select, recv_q, "srk,rktf->stf").reshape(tok_rows, query_width)
    def step_over(value, hops):
        return lax.ppermute(
            value, "inner", [(i, (i + 2 * hops) % group_width) for i in range(group_width)]
        )

    from_left = step_over(pair, 1)
    from_right = step_over(pair, -1)
    relayed = jnp.stack([step_over(from_left[0], 1), step_over(from_right[1], -1)])
    gathered = jnp.concatenate([pair, from_left, relayed, from_right])
    entry = jnp.arange(group_width, dtype=jnp.int32)
    inner_of = ((my_index - 2 * (entry // 2)) % group_width) ^ (entry % 2)
    parity = outer_index % 2
    offer = lax.dynamic_slice_in_dim(gathered, parity, len(partner_steps), axis=1)
    outer_count = lax.axis_size("outer")
    partner_pairs = [(o, o ^ 1) for o in range(outer_count)]
    received = lax.ppermute(offer, "outer", partner_pairs)
    sources = [(gathered, own_steps), (received, partner_steps)]
    key_device, key_first, key_last = [], [], []
    for array, steps in sources:
        for slot, step in enumerate(steps):
            key_device.append(
                (outer_index - step) * group_width + inner_of
            )
            key_first.append(array[:, slot, tok_rows, 0])
            key_last.append(array[:, slot, tok_rows + seg_rows - 1, pair_width - 1])
    key_device = jnp.concatenate(key_device)
    key_first = jnp.concatenate(key_first)
    key_last = jnp.concatenate(key_last)
    first_seg = segment_ids[0].astype(jnp.bfloat16)
    last_seg = segment_ids[tok_rows - 1].astype(jnp.bfloat16)
    needed = (
        (key_device >= 0)
        & (key_device <= owner_index)
        & (key_last >= first_seg)
        & (key_first <= last_seg)
    )
    whole = (
        (key_device < owner_index)
        & (key_first == key_last)
        & (key_first == first_seg)
        & (first_seg == last_seg)
    )
    needed = jnp.where(needed, jnp.where(whole, 1, 2), 0).astype(jnp.int32)
    meta = jnp.concatenate([owner_index.reshape(1).astype(jnp.int32), needed, key_device])
    query_seg = segment_ids.astype(jnp.float32).reshape(tok_rows, 1)
    return attend(meta, q_seq, query_seg, gathered, received, head_count, head_size, score_scale)


def attend(meta, q_seq, query_seg, gathered, received, head_count, head_size, score_scale):
    tok_rows = q_seq.shape[0]
    group_width, first_slots, packed_rows, pair_width = gathered.shape
    second_slots = received.shape[1]
    first_count = group_width * first_slots
    block_count = first_count + group_width * second_slots
    seg_rows = tok_rows // pair_width

    def kernel(meta_ref, q_ref, qseg_ref, first_ref, second_ref, out_ref, m_ref, l_ref, acc_ref):
        b = pl.program_id(0)

        @pl.when(b == 0)
        def _():
            m_ref[...] = jnp.full(m_ref.shape, -1e30, jnp.float32)
            l_ref[...] = jnp.zeros(l_ref.shape, jnp.float32)
            acc_ref[...] = jnp.zeros(acc_ref.shape, jnp.float32)

        def absorb(kv_ref, masked_block):
            keys = kv_ref[0, 0, :tok_rows, :head_size]
            values = kv_ref[0, 0, :tok_rows, head_size:]
            if masked_block:
                own = meta_ref[0]
                device = meta_ref[1 + block_count + b]
                seg_parts = [
                    kv_ref[0, 0, tok_rows + r : tok_rows + r + 1, :].astype(jnp.float32)
                    for r in range(seg_rows)
                ]
                key_seg = jnp.concatenate(seg_parts, axis=1)
                key_pos = device * tok_rows + lax.broadcasted_iota(jnp.int32, (1, tok_rows), 1)
                query_pos = own * tok_rows + lax.broadcasted_iota(jnp.int32, (tok_rows, 1), 0)
                visible = (key_pos <= query_pos) & (key_seg == qseg_ref[...])
            for h in range(head_count):
                queries = q_ref[:, h * head_size : (h + 1) * head_size]
                scores = lax.dot_general(
                    queries, keys, (((1,), (1,)), ((), ())), preferred_element_type=jnp.float32
                )
                if masked_block:
                    scores = jnp.where(visible, scores, -1e30)
                m_prev = m_ref[h]
                m_next = jnp.maximum(m_prev, jnp.max(scores, axis=1, keepdims=True))
                factor = jnp.exp((m_prev - m_next) * score_scale)
                m_row = m_next[:, :1]
                if masked_block:
                    m_row = jnp.where(m_row == -1e30, 0.0, m_row)
                weights = jnp.exp((scores - m_row) * score_scale)
                l_ref[h] = l_ref[h] * factor + jnp.sum(weights, axis=1, keepdims=True)
                acc_ref[h] = acc_ref[h] * factor + jnp.dot(
                    weights.astype(jnp.bfloat16), values, preferred_element_type=jnp.float32
                )
                m_ref[h] = m_next

        mode = meta_ref[1 + b]
        for ref, in_range in ((first_ref, b < first_count), (second_ref, b >= first_count)):
            for masked_block, code in ((False, 1), (True, 2)):
                @pl.when(in_range & (mode == code))
                def _(ref=ref, masked_block=masked_block):
                    absorb(ref, masked_block)

        @pl.when(b == block_count - 1)
        def _():
            for h in range(head_count):
                out_ref[:, h * head_size : (h + 1) * head_size] = (
                    acc_ref[h] / l_ref[h]
                ).astype(out_ref.dtype)

    def first_map(b, meta):
        c = jnp.minimum(b, first_count - 1)
        return (c % group_width, c // group_width, 0, 0)

    def second_map(b, meta):
        c = jnp.maximum(b - first_count, 0)
        return (c % group_width, c // group_width, 0, 0)

    grid_spec = pltpu.PrefetchScalarGridSpec(
        num_scalar_prefetch=1,
        grid=(block_count,),
        in_specs=[
            pl.BlockSpec(q_seq.shape, lambda b, meta: (0, 0)),
            pl.BlockSpec(query_seg.shape, lambda b, meta: (0, 0)),
            pl.BlockSpec((1, 1, packed_rows, pair_width), first_map),
            pl.BlockSpec((1, 1, packed_rows, pair_width), second_map),
        ],
        out_specs=pl.BlockSpec(q_seq.shape, lambda b, meta: (0, 0)),
        scratch_shapes=[
            pltpu.VMEM((head_count, tok_rows, head_size), jnp.float32),
            pltpu.VMEM((head_count, tok_rows, head_size), jnp.float32),
            pltpu.VMEM((head_count, tok_rows, head_size), jnp.float32),
        ],
    )
    flops = 4 * block_count * tok_rows * tok_rows * head_size * head_count
    return pl.pallas_call(
        kernel,
        grid_spec=grid_spec,
        out_shape=jax.ShapeDtypeStruct(q_seq.shape, q_seq.dtype),
        compiler_params=pltpu.CompilerParams(dimension_semantics=("arbitrary",)),
        cost_estimate=pl.CostEstimate(
            flops=flops,
            transcendentals=block_count * tok_rows * tok_rows * head_count,
            bytes_accessed=(gathered.size + received.size) * 2 + q_seq.size * 4,
        ),
    )(meta, q_seq, query_seg, gathered, received)


def solution(mesh):
    in_specs = (
        P(("outer", "inner"), None),
        P(("outer", "inner"), None),
        P("outer", None),
        P("outer"),
        P(("outer", "inner")),
    )
    out_specs = P(("outer", "inner"), None)
    return jax.shard_map(local, mesh=mesh, in_specs=in_specs, out_specs=out_specs, check_vma=False)
```

profile of v0, /device:TPU:70, one launch (start us, length us, event | category | flops | bytes accessed | tf_op | source)
XLA Modules:
  0.0 251.7 jit_solution(5414577414431968000)
XLA Ops:
  0.0 0.0 copy-start
  0.0 0.8 add_select_fusion
  0.8 0.7 and_reduce_fusion.1
  1.5 0.3 convert_reduce_fusion
  1.8 0.8 select_reduce_fusion
  2.6 1.4 fusion.1
  4.0 0.9 copy.25
  4.9 5.8 %all-to-all-start = ((bf16[8,1,128,256]{3,2,1,0:T(8,128)(2,1)}), bf16[8,1,128,256]{3,2,1,0:T(8,128)(2,1)S(1)}, u32[]{:S(2)}, u32[]{:S(2)}) async-start(bf16[8,1,128,256]{3,2,1,0:T(8,128)(2,1)} %copy.25), calls=%async_computation | async-start | bytes 1048576 | tf_op jit(solution)/shard_map/all_to_all | solution.py:58
  10.8 0.8 fusion.29
  11.6 0.1 pad.7.clone
  11.7 0.9 and_reduce_fusion
  12.6 5.6 %all-to-all-done = bf16[8,1,128,256]{3,2,1,0:T(8,128)(2,1)S(1)} async-done(((bf16[8,1,128,256]{3,2,1,0:T(8,128)(2,1)}), bf16[8,1,128,256]{3,2,1,0:T(8,128)(2,1)S(1)}, u32[]{:S(2)}, u32[]{:S(2)}) %all-to-all-start) | async-done | bytes 524320 | tf_op jit(solution)/shard_map/all_to_all | solution.py:58
  18.2 0.4 convolution_convert_fusion.3
  18.6 0.1 fusion.27
  18.8 0.0 copy-start.2
  18.8 5.1 %collective-permute-start.1 = (bf16[528,256]{1,0:T(8,128)(2,1)S(1)}, bf16[528,256]{1,0:T(8,128)(2,1)S(1)}, u32[]{:S(2)}, u32[]{:S(2)}) collective-permute-start(bf16[528,256]{1,0:T(8,128)(2,1)S(1)} %get-tuple-element.22), channel_id=1, source_target_pairs={{0,32},{8,40},{16,48},{24,56},{32,64},{40,72},{48,80},{56,88},{64,... | collective-permute-start | bytes 811016 | tf_op jit(solution)/shard_map/ppermute | solution.py:14
  23.9 2.6 %collective-permute-start = (bf16[528,256]{1,0:T(8,128)(2,1)S(1)}, bf16[528,256]{1,0:T(8,128)(2,1)S(1)}, u32[]{:S(2)}, u32[]{:S(2)}) collective-permute-start(bf16[528,256]{1,0:T(8,128)(2,1)S(1)} %get-tuple-element.22), channel_id=1, source_target_pairs={{0,16},{8,24},{16,32},{24,40},{32,48},{40,56},{48,64},{56,72},{64,... | collective-permute-start | bytes 811016 | tf_op jit(solution)/shard_map/ppermute | solution.py:14
  26.5 7.0 %collective-permute-done.1 = bf16[528,256]{1,0:T(8,128)(2,1)S(1)} collective-permute-done((bf16[528,256]{1,0:T(8,128)(2,1)S(1)}, bf16[528,256]{1,0:T(8,128)(2,1)S(1)}, u32[]{:S(2)}, u32[]{:S(2)}) %collective-permute-start.1) | collective-permute-done | bytes 270368 | tf_op jit(solution)/shard_map/ppermute | solution.py:14
  33.5 4.3 %collective-permute-done = bf16[528,256]{1,0:T(8,128)(2,1)S(1)} collective-permute-done((bf16[528,256]{1,0:T(8,128)(2,1)S(1)}, bf16[528,256]{1,0:T(8,128)(2,1)S(1)}, u32[]{:S(2)}, u32[]{:S(2)}) %collective-permute-start) | collective-permute-done | bytes 270368 | tf_op jit(solution)/shard_map/ppermute | solution.py:14
  37.8 0.1 fusion.28
  38.0 1.3 collective-permute-start.2
  39.2 17.4 %collective-permute-done.2 = bf16[3,528,256]{2,1,0:T(8,128)(2,1)S(1)} collective-permute-done((bf16[3,528,256]{2,1,0:T(8,128)(2,1)S(1)}, bf16[3,528,256]{2,1,0:T(8,128)(2,1)S(1)}, u32[]{:S(2)}, u32[]{:S(2)}) %collective-permute-start.2) | collective-permute-done | bytes 811040 | tf_op jit(solution)/shard_map/ppermute | solution.py:84
  56.7 0.0 copy-done.2
  56.7 0.0 copy-done.3
  56.7 0.0 copy-done.4
  56.7 1.3 pad_maximum_fusion
  58.0 2.3 collective-permute-start.3
  60.3 0.0 collective-permute-start.5
  60.3 33.7 %collective-permute-done.3 = bf16[2,3,528,256]{3,2,1,0:T(8,128)(2,1)} collective-permute-done((bf16[2,3,528,256]{3,2,1,0:T(8,128)(2,1)}, bf16[2,3,528,256]{3,2,1,0:T(8,128)(2,1)}, u32[]{:S(2)}, u32[]{:S(2)}) %collective-permute-start.3) | collective-permute-done | bytes 1622048 | tf_op jit(solution)/shard_map/ppermute | solution.py:90
  94.0 1.2 slice_bitcast_fusion.1
  95.2 3.1 %collective-permute-start.4 = (bf16[3,528,256]{2,1,0:T(8,128)(2,1)S(1)}, bf16[3,528,256]{2,1,0:T(8,128)(2,1)S(1)}, u32[]{:S(2)}, u32[]{:S(2)}) collective-permute-start(bf16[3,528,256]{2,1,0:T(8,128)(2,1)S(1)} %slice_bitcast_fusion.1), channel_id=1, source_target_pairs={{0,2},{1,3},{2,4},{3,5},{4,6},{5,7},{6,0},{7,1},{8,10},{9,11},{10,... | collective-permute-start | bytes 2433032 | tf_op jit(solution)/shard_map/ppermute | solution.py:90
  98.2 0.0 collective-permute-done.5
  98.2 0.1 slice_bitcast_fusion
  98.3 0.1 collective-permute-start.6
  98.4 1.2 constant_dynamic-update-slice_fusion.3
  99.6 0.1 constant_dynamic-update-slice_fusion.2
  99.6 1.5 constant_dynamic-update-slice_fusion.1
  101.2 11.6 %collective-permute-done.4 = bf16[3,528,256]{2,1,0:T(8,128)(2,1)S(1)} collective-permute-done((bf16[3,528,256]{2,1,0:T(8,128)(2,1)S(1)}, bf16[3,528,256]{2,1,0:T(8,128)(2,1)S(1)}, u32[]{:S(2)}, u32[]{:S(2)}) %collective-permute-start.4) | collective-permute-done | bytes 811040 | tf_op jit(solution)/shard_map/ppermute | solution.py:90
  112.8 0.1 bitcast_dynamic-update-slice_fusion.1
  112.8 3.3 %collective-permute-done.6 = bf16[3,528,256]{2,1,0:T(8,128)(2,1)S(1)} collective-permute-done((bf16[3,528,256]{2,1,0:T(8,128)(2,1)S(1)}, bf16[3,528,256]{2,1,0:T(8,128)(2,1)S(1)}, u32[]{:S(2)}, u32[]{:S(2)}) %collective-permute-start.6) | collective-permute-done | bytes 811040 | tf_op jit(solution)/shard_map/ppermute | solution.py:90
  116.2 0.1 bitcast_dynamic-update-slice_fusion
  116.2 0.1 constant_dynamic-update-slice_fusion.first_ref
  116.3 0.0 copy-start.1
  116.4 2.6 %constant_dynamic-slice_fusion = bf16[8,2,528,256]{3,2,1,0:T(8,128)(2,1)} fusion(bf16[8,3,528,256]{3,2,1,0:T(8,128)(2,1)S(1)} %constant_dynamic-update-slice_fusion.first_ref, s32[]{:T(128)S(6)} %select_n.52), kind=kLoop, calls=%fused_computation.81 | loop fusion | bytes 8650756 | tf_op jit(solution)/shard_map/dynamic_slice | solution.py:101
  119.0 0.0 collective-permute-start.7
  119.0 1.4 copy-done.1
  120.3 0.0 copy-done
  120.4 0.7 fusion
  121.1 1.3 copy.29
  122.4 4.5 %all-to-all-start.1 = ((bf16[8,1,128,512]{3,2,1,0:T(8,128)(2,1)}), bf16[8,1,128,512]{3,2,1,0:T(8,128)(2,1)S(1)}, u32[]{:S(2)}, u32[]{:S(2)}) async-start(bf16[8,1,128,512]{3,2,1,0:T(8,128)(2,1)} %copy.29), calls=%async_computation.1 | async-start | bytes 2097152 | tf_op jit(solution)/shard_map/all_to_all | solution.py:87
  126.9 0.9 copy.32.qseg_ref
  127.8 0.6 fusion.30
  129.6 0.1 concatenate.20
  129.7 9.6 %all-to-all-done.1 = bf16[8,1,128,512]{3,2,1,0:T(8,128)(2,1)S(1)} async-done(((bf16[8,1,128,512]{3,2,1,0:T(8,128)(2,1)}), bf16[8,1,128,512]{3,2,1,0:T(8,128)(2,1)S(1)}, u32[]{:S(2)}, u32[]{:S(2)}) %all-to-all-start.1) | async-done | bytes 1048608 | tf_op jit(solution)/shard_map/all_to_all | solution.py:87
  139.3 0.7 convolution_convert_fusion.1
  140.0 0.9 copy.31
  140.9 1.0 slice_reduce_fusion.7
  141.9 0.0 collective-permute-done.7.second_ref
  142.0 1.0 slice_reduce_fusion.5
  143.0 0.1 concatenate.23
  143.1 0.1 concatenate.24
  143.2 1.2 and_select_fusion.1
  144.3 0.6 concatenate.25.meta_ref
  144.9 106.8 %shard_map.55 = bf16[512,512]{1,0:T(8,128)(2,1)} custom-call(s32[81]{0:T(128)} %concatenate.25.meta_ref, bf16[512,512]{1,0:T(8,128)(2,1)} %bitcast.54, f32[512,1]{1,0:T(8,128)} %copy.32.qseg_ref, bf16[8,3,528,256]{3,2,1,0:T(8,128)(2,1)} %copy-done.1, bf16[8,2,528,256]{3,2,1,0:T(8,128)(2,1)} %collective-permute-done.7.second_ref), custom_call_target="tpu_custom_call" | custom-call | flops 21474836480 | bytes 11862016 | tf_op jit(solution)/shard_map/pallas_call | solution.py:227
  (12 shorter events, 0.1 us)
Async XLA Ops:
  0.0 120.3 %copy-start = (bf16[1024,512]{1,0:T(8,128)(2,1)S(1)}, bf16[1024,512]{1,0:T(8,128)(2,1)}, u32[]{:S(2)}) copy-start(bf16[1024,512]{1,0:T(8,128)(2,1)} %param.5) | copy-start | bytes 3145732
  4.9 13.2 %all-to-all-start = ((bf16[8,1,128,256]{3,2,1,0:T(8,128)(2,1)}), bf16[8,1,128,256]{3,2,1,0:T(8,128)(2,1)S(1)}, u32[]{:S(2)}, u32[]{:S(2)}) async-start(bf16[8,1,128,256]{3,2,1,0:T(8,128)(2,1)} %copy.25), calls=%async_computation | async-start | bytes 1048576 | tf_op jit(solution)/shard_map/all_to_all | solution.py:58
  18.8 37.9 %copy-start.2 = (bf16[1,528,256]{2,1,0:T(8,128)(2,1)}, bf16[1,528,256]{2,1,0:T(8,128)(2,1)S(1)}, u32[]{:S(2)}) copy-start(bf16[1,528,256]{2,1,0:T(8,128)(2,1)S(1)} %get-tuple-element.21) | copy-start | bytes 811012
  18.8 14.7 %collective-permute-start.1 = (bf16[528,256]{1,0:T(8,128)(2,1)S(1)}, bf16[528,256]{1,0:T(8,128)(2,1)S(1)}, u32[]{:S(2)}, u32[]{:S(2)}) collective-permute-start(bf16[528,256]{1,0:T(8,128)(2,1)S(1)} %get-tuple-element.22), channel_id=1, source_target_pairs={{0,32},{8,40},{16,48},{24,56},{32,64},{40,72},{48,80},{56,88},{64,... | collective-permute-start | bytes 811016 | tf_op jit(solution)/shard_map/ppermute | solution.py:14
  23.9 13.9 %collective-permute-start = (bf16[528,256]{1,0:T(8,128)(2,1)S(1)}, bf16[528,256]{1,0:T(8,128)(2,1)S(1)}, u32[]{:S(2)}, u32[]{:S(2)}) collective-permute-start(bf16[528,256]{1,0:T(8,128)(2,1)S(1)} %get-tuple-element.22), channel_id=1, source_target_pairs={{0,16},{8,24},{16,32},{24,40},{32,48},{40,56},{48,64},{56,72},{64,... | collective-permute-start | bytes 811016 | tf_op jit(solution)/shard_map/ppermute | solution.py:14
  33.5 23.1 %copy-start.3 = (bf16[528,256]{1,0:T(8,128)(2,1)}, bf16[528,256]{1,0:T(8,128)(2,1)S(1)}, u32[]{:S(2)}) copy-start(bf16[528,256]{1,0:T(8,128)(2,1)S(1)} %collective-permute-done.1) | copy-start | bytes 811012
  37.8 18.8 %copy-start.4 = (bf16[528,256]{1,0:T(8,128)(2,1)}, bf16[528,256]{1,0:T(8,128)(2,1)S(1)}, u32[]{:S(2)}) copy-start(bf16[528,256]{1,0:T(8,128)(2,1)S(1)} %collective-permute-done) | copy-start | bytes 811012
  38.0 18.7 %collective-permute-start.2 = (bf16[3,528,256]{2,1,0:T(8,128)(2,1)S(1)}, bf16[3,528,256]{2,1,0:T(8,128)(2,1)S(1)}, u32[]{:S(2)}, u32[]{:S(2)}) collective-permute-start(bf16[3,528,256]{2,1,0:T(8,128)(2,1)S(1)} %get-tuple-element.20), channel_id=1, source_target_pairs={{0,1},{1,0},{2,3},{3,2},{4,5},{5,4},{6,7},{7,6},{8,9},{9,8},{10,11... | collective-permute-start | bytes 2433032 | tf_op jit(solution)/shard_map/ppermute | solution.py:84
  58.0 36.0 %collective-permute-start.3 = (bf16[2,3,528,256]{3,2,1,0:T(8,128)(2,1)}, bf16[2,3,528,256]{3,2,1,0:T(8,128)(2,1)}, u32[]{:S(2)}, u32[]{:S(2)}) collective-permute-start(bf16[2,3,528,256]{3,2,1,0:T(8,128)(2,1)} %pad_maximum_fusion), channel_id=1, source_target_pairs={{0,2},{1,3},{2,4},{3,5},{4,6},{5,7},{6,0},{7,1},{8,10},{9,11},{10,... | collective-permute-start | bytes 4866056 | tf_op jit(solution)/shard_map/ppermute | solution.py:90
  60.3 38.0 %collective-permute-start.5 = (bf16[2,3,528,256]{3,2,1,0:T(8,128)(2,1)}, bf16[2,3,528,256]{3,2,1,0:T(8,128)(2,1)S(1)}, u32[]{:S(2)}, u32[]{:S(2)}) collective-permute-start(bf16[2,3,528,256]{3,2,1,0:T(8,128)(2,1)} %pad_maximum_fusion), channel_id=1, source_target_pairs={{0,6},{1,7},{2,0},{3,1},{4,2},{5,3},{6,4},{7,5},{8,14},{9,15},{10,... | collective-permute-start | bytes 4866056 | tf_op jit(solution)/shard_map/ppermute | solution.py:90
  95.2 17.6 %collective-permute-start.4 = (bf16[3,528,256]{2,1,0:T(8,128)(2,1)S(1)}, bf16[3,528,256]{2,1,0:T(8,128)(2,1)S(1)}, u32[]{:S(2)}, u32[]{:S(2)}) collective-permute-start(bf16[3,528,256]{2,1,0:T(8,128)(2,1)S(1)} %slice_bitcast_fusion.1), channel_id=1, source_target_pairs={{0,2},{1,3},{2,4},{3,5},{4,6},{5,7},{6,0},{7,1},{8,10},{9,11},{10,... | collective-permute-start | bytes 2433032 | tf_op jit(solution)/shard_map/ppermute | solution.py:90
  98.3 17.9 %collective-permute-start.6 = (bf16[3,528,256]{2,1,0:T(8,128)(2,1)S(1)}, bf16[3,528,256]{2,1,0:T(8,128)(2,1)S(1)}, u32[]{:S(2)}, u32[]{:S(2)}) collective-permute-start(bf16[3,528,256]{2,1,0:T(8,128)(2,1)S(1)} %slice_bitcast_fusion), channel_id=1, source_target_pairs={{0,6},{1,7},{2,0},{3,1},{4,2},{5,3},{6,4},{7,5},{8,14},{9,15},{10,... | collective-permute-start | bytes 2433032 | tf_op jit(solution)/shard_map/ppermute | solution.py:90
  116.3 4.0 %copy-start.1 = (bf16[8,3,528,256]{3,2,1,0:T(8,128)(2,1)}, bf16[8,3,528,256]{3,2,1,0:T(8,128)(2,1)S(1)}, u32[]{:S(2)}) copy-start(bf16[8,3,528,256]{3,2,1,0:T(8,128)(2,1)S(1)} %constant_dynamic-update-slice_fusion.first_ref) | copy-start | bytes 19464196
  119.0 23.0 %collective-permute-start.7 = (bf16[8,2,528,256]{3,2,1,0:T(8,128)(2,1)}, bf16[8,2,528,256]{3,2,1,0:T(8,128)(2,1)}, u32[]{:S(2)}, u32[]{:S(2)}) collective-permute-start(bf16[8,2,528,256]{3,2,1,0:T(8,128)(2,1)} %constant_dynamic-slice_fusion), channel_id=1, source_target_pairs={{0,8},{8,0},{16,24},{24,16},{32,40},{40,32},{48,56},{56,48},{64,72... | collective-permute-start | bytes 12976136 | tf_op jit(solution)/shard_map/ppermute | solution.py:104
  122.4 16.9 %all-to-all-start.1 = ((bf16[8,1,128,512]{3,2,1,0:T(8,128)(2,1)}), bf16[8,1,128,512]{3,2,1,0:T(8,128)(2,1)S(1)}, u32[]{:S(2)}, u32[]{:S(2)}) async-start(bf16[8,1,128,512]{3,2,1,0:T(8,128)(2,1)} %copy.29), calls=%async_computation.1 | async-start | bytes 2097152 | tf_op jit(solution)/shard_map/all_to_all | solution.py:87
where the time goes:
time: 251 us; the launch traced here: 252 us
  Pallas kernels  107 us (43%)
  waiting for transfers between devices  92.7 us (37%)
  starting transfers between devices  24.7 us (10%)
  local copies, waits for them, and re-layouts  14.7 us (6%)
  other arithmetic  8.23 us (3%)
  matrix products  3.27 us (1%)
    pallas_call x1, Pallas kernels, attend(): pl.pallas_call(kernel, grid_spec=grid_spec, out_shape=jax.ShapeDtypeStruc...  107 us
    ppermute x4, waiting for transfers between devices, step_over(): lax.ppermute(value, 'inner', [(i, (i + 2 * hops) % group_width) for i in...  48.7 us
    ppermute x1, waiting for transfers between devices, local(): lax.ppermute(own_stack, 'inner', [(i, i ^ 1) for i in range(group_width)])  17.4 us
    ppermute x2, waiting for transfers between devices, shifted(): lax.ppermute(value, axis, [(source, source + steps) for source in range(l...  11.3 us
    all_to_all x1, waiting for transfers between devices, local(): lax.all_to_all(send_q, 'inner', split_axis=0, concat_axis=0, tiled=True)  9.6 us
    ppermute x2, starting transfers between devices, shifted(): lax.ppermute(value, axis, [(source, source + steps) for source in range(l...  7.69 us
    all_to_all x1, starting transfers between devices, local(): lax.all_to_all(send_kv, 'inner', split_axis=0, concat_axis=0, tiled=True)  5.84 us
    all_to_all x1, waiting for transfers between devices, local(): lax.all_to_all(send_kv, 'inner', split_axis=0, concat_axis=0, tiled=True)  5.64 us
  transfers between devices with their start and end apart: 10, of which 8 were waited for; matrix products, arithmetic and copies ran while one was open for 5% of the time, Pallas kernels for 0%

commit v1 on v0

--- a/solution.py
+++ b/solution.py
@@ -85,7 +85,6 @@
     pair = jnp.stack([own_stack, pair_mate])
     send_q = lax.optimization_barrier((send_q, pair_mate))[0]
     recv_q = lax.all_to_all(send_q, "inner", split_axis=0, concat_axis=0, tiled=True)
-    q_seq = select_rows(take_select, recv_q, "srk,rktf->stf").reshape(tok_rows, query_width)
     def step_over(value, hops):
         return lax.ppermute(
             value, "inner", [(i, (i + 2 * hops) % group_width) for i in range(group_width)]
@@ -93,8 +92,10 @@
 
     from_left = step_over(pair, 1)
     from_right = step_over(pair, -1)
-    relayed = jnp.stack([step_over(from_left[0], 1), step_over(from_right[1], -1)])
+    left_half, right_half, recv_q = lax.optimization_barrier((from_left[0], from_right[1], recv_q))
+    relayed = jnp.stack([step_over(left_half, 1), step_over(right_half, -1)])
     gathered = jnp.concatenate([pair, from_left, relayed, from_right])
+    q_seq = select_rows(take_select, recv_q, "srk,rktf->stf").reshape(tok_rows, query_width)
     entry = jnp.arange(group_width, dtype=jnp.int32)
     inner_of = ((my_index - 2 * (entry // 2)) % group_width) ^ (entry % 2)
     parity = outer_index % 2

time: 251 us -> 250 us (level)
  the two profiles are of different devices: /device:TPU:70 before, /device:TPU:79 now
where the time goes in v1:
time: 250 us; the launch traced here: 247 us
  Pallas kernels  107 us (43%)
  waiting for transfers between devices  79.8 us (32%)
  starting transfers between devices  27 us (11%)
  local copies, waits for them, and re-layouts  21.2 us (8%)
  other arithmetic  8.1 us (3%)
  matrix products  3.27 us (1%)
    pallas_call x1, Pallas kernels, attend(): pl.pallas_call(kernel, grid_spec=grid_spec, out_shape=jax.ShapeDtypeStruc...  107 us
    ppermute x4, waiting for transfers between devices, step_over(): lax.ppermute(value, 'inner', [(i, (i + 2 * hops) % group_width) for i in...  37.3 us
    ppermute x1, waiting for transfers between devices, local(): lax.ppermute(own_stack, 'inner', [(i, i ^ 1) for i in range(group_width)])  17.4 us
    ppermute x2, waiting for transfers between devices, shifted(): lax.ppermute(value, axis, [(source, source + steps) for source in range(l...  10.8 us
    all_to_all x1, waiting for transfers between devices, local(): lax.all_to_all(send_q, 'inner', split_axis=0, concat_axis=0, tiled=True)  7.43 us
    all_to_all x1, starting transfers between devices, local(): lax.all_to_all(send_q, 'inner', split_axis=0, concat_axis=0, tiled=True)  6.17 us
    ppermute x2, starting transfers between devices, shifted(): lax.ppermute(value, axis, [(source, source + steps) for source in range(l...  5.84 us
    ppermute x1, starting transfers between devices, local(): received = lax.ppermute(offer, 'outer', partner_pairs)  5.63 us
  transfers between devices with their start and end apart: 10, of which 10 were waited for; matrix products, arithmetic and copies ran while one was open for 6% of the time, Pallas kernels for 0%

profile of v1, /device:TPU:79, one launch (start us, length us, event | category | flops | bytes accessed | tf_op | source)
XLA Modules:
  0.0 247.5 jit_solution(7324874334307688943)
XLA Ops:
  0.0 0.0 copy-start
  0.0 0.8 add_select_fusion
  0.8 0.7 and_reduce_fusion.1
  1.5 0.3 convert_reduce_fusion
  1.8 0.8 select_reduce_fusion
  2.6 1.4 fusion.1
  4.0 0.9 copy.25
  4.9 5.3 %all-to-all-start = ((bf16[8,1,128,256]{3,2,1,0:T(8,128)(2,1)}), bf16[8,1,128,256]{3,2,1,0:T(8,128)(2,1)S(1)}, u32[]{:S(2)}, u32[]{:S(2)}) async-start(bf16[8,1,128,256]{3,2,1,0:T(8,128)(2,1)} %copy.25), calls=%async_computation | async-start | bytes 1048576 | tf_op jit(solution)/shard_map/all_to_all | solution.py:58
  10.2 0.8 fusion.28
  11.0 0.1 pad.7.clone
  11.1 0.9 and_reduce_fusion
  12.0 5.0 %all-to-all-done = bf16[8,1,128,256]{3,2,1,0:T(8,128)(2,1)S(1)} async-done(((bf16[8,1,128,256]{3,2,1,0:T(8,128)(2,1)}), bf16[8,1,128,256]{3,2,1,0:T(8,128)(2,1)S(1)}, u32[]{:S(2)}, u32[]{:S(2)}) %all-to-all-start) | async-done | bytes 524320 | tf_op jit(solution)/shard_map/all_to_all | solution.py:58
  17.0 0.4 convolution_convert_fusion.3
  17.4 0.1 fusion.26
  17.6 3.9 %collective-permute-start.1 = (bf16[528,256]{1,0:T(8,128)(2,1)S(1)}, bf16[528,256]{1,0:T(8,128)(2,1)S(1)}, u32[]{:S(2)}, u32[]{:S(2)}) collective-permute-start(bf16[528,256]{1,0:T(8,128)(2,1)S(1)} %get-tuple-element.28), channel_id=1, source_target_pairs={{0,32},{8,40},{16,48},{24,56},{32,64},{40,72},{48,80},{56,88},{64,... | collective-permute-start | bytes 811016 | tf_op jit(solution)/shard_map/ppermute | solution.py:14
  21.5 1.9 collective-permute-start
  23.4 6.0 %collective-permute-done.1 = bf16[528,256]{1,0:T(8,128)(2,1)S(1)} collective-permute-done((bf16[528,256]{1,0:T(8,128)(2,1)S(1)}, bf16[528,256]{1,0:T(8,128)(2,1)S(1)}, u32[]{:S(2)}, u32[]{:S(2)}) %collective-permute-start.1) | collective-permute-done | bytes 270368 | tf_op jit(solution)/shard_map/ppermute | solution.py:14
  29.5 4.8 %collective-permute-done = bf16[528,256]{1,0:T(8,128)(2,1)S(1)} collective-permute-done((bf16[528,256]{1,0:T(8,128)(2,1)S(1)}, bf16[528,256]{1,0:T(8,128)(2,1)S(1)}, u32[]{:S(2)}, u32[]{:S(2)}) %collective-permute-start) | collective-permute-done | bytes 270368 | tf_op jit(solution)/shard_map/ppermute | solution.py:14
  34.3 0.0 copy-start.2
  34.3 0.1 fusion.27
  34.4 0.7 collective-permute-start.2
  35.0 17.4 %collective-permute-done.2 = bf16[3,528,256]{2,1,0:T(8,128)(2,1)S(1)} collective-permute-done((bf16[3,528,256]{2,1,0:T(8,128)(2,1)S(1)}, bf16[3,528,256]{2,1,0:T(8,128)(2,1)S(1)}, u32[]{:S(2)}, u32[]{:S(2)}) %collective-permute-start.2) | collective-permute-done | bytes 811040 | tf_op jit(solution)/shard_map/ppermute | solution.py:84
  52.5 0.0 copy-done.2
  52.5 1.3 pad_maximum_fusion
  53.8 1.9 collective-permute-start.3
  55.7 0.0 collective-permute-start.4
  55.7 0.0 copy-done
  55.7 0.7 fusion
  56.4 1.3 copy.29
  57.8 6.2 %all-to-all-start.1 = ((bf16[8,1,128,512]{3,2,1,0:T(8,128)(2,1)}), bf16[8,1,128,512]{3,2,1,0:T(8,128)(2,1)S(1)}, u32[]{:S(2)}, u32[]{:S(2)}) async-start(bf16[8,1,128,512]{3,2,1,0:T(8,128)(2,1)} %copy.29), calls=%async_computation.1 | async-start | bytes 2097152 | tf_op jit(solution)/shard_map/all_to_all | solution.py:87
  63.9 24.6 %collective-permute-done.3 = bf16[2,3,528,256]{3,2,1,0:T(8,128)(2,1)} collective-permute-done((bf16[2,3,528,256]{3,2,1,0:T(8,128)(2,1)}, bf16[2,3,528,256]{3,2,1,0:T(8,128)(2,1)}, u32[]{:S(2)}, u32[]{:S(2)}) %collective-permute-start.3) | collective-permute-done | bytes 1622048 | tf_op jit(solution)/shard_map/ppermute | solution.py:89
  88.6 2.1 slice_bitcast_fusion.1
  90.7 0.7 collective-permute-done.4
  91.4 2.1 slice_bitcast_fusion
  93.5 7.4 %all-to-all-done.1 = bf16[8,1,128,512]{3,2,1,0:T(8,128)(2,1)S(1)} async-done(((bf16[8,1,128,512]{3,2,1,0:T(8,128)(2,1)}), bf16[8,1,128,512]{3,2,1,0:T(8,128)(2,1)S(1)}, u32[]{:S(2)}, u32[]{:S(2)}) %all-to-all-start.1) | async-done | bytes 1048608 | tf_op jit(solution)/shard_map/all_to_all | solution.py:87
  101.0 0.9 collective-permute-start.5
  101.8 0.6 collective-permute-start.6
  102.4 1.0 constant_dynamic-update-slice_fusion.3
  103.4 0.1 constant_dynamic-update-slice_fusion.2
  103.5 1.5 constant_dynamic-update-slice_fusion.1
  105.0 10.5 %collective-permute-done.5 = bf16[3,528,256]{2,1,0:T(8,128)(2,1)} collective-permute-done((bf16[3,528,256]{2,1,0:T(8,128)(2,1)}, bf16[3,528,256]{2,1,0:T(8,128)(2,1)}, u32[]{:S(2)}, u32[]{:S(2)}) %collective-permute-start.5) | collective-permute-done | bytes 811040 | tf_op jit(solution)/shard_map/ppermute | solution.py:89
  115.5 1.2 bitcast_dynamic-update-slice_fusion.1
  116.7 1.4 collective-permute-done.6
  118.1 0.1 bitcast_dynamic-update-slice_fusion
  118.1 1.5 constant_dynamic-update-slice_fusion.first_ref
  119.7 0.0 copy-start.1
  119.7 2.7 %copy-done.1 = bf16[8,3,528,256]{3,2,1,0:T(8,128)(2,1)} copy-done((bf16[8,3,528,256]{3,2,1,0:T(8,128)(2,1)}, bf16[8,3,528,256]{3,2,1,0:T(8,128)(2,1)S(1)}, u32[]{:S(2)}) %copy-start.1) | copy-done | bytes 6488088
  122.4 2.4 constant_dynamic-slice_fusion
  124.8 5.6 %collective-permute-start.7 = (bf16[8,2,528,256]{3,2,1,0:T(8,128)(2,1)}, bf16[8,2,528,256]{3,2,1,0:T(8,128)(2,1)}, u32[]{:S(2)}, u32[]{:S(2)}) collective-permute-start(bf16[8,2,528,256]{3,2,1,0:T(8,128)(2,1)} %constant_dynamic-slice_fusion), channel_id=1, source_target_pairs={{0,8},{8,0},{16,24},{24,16},{32,40},{40,32},{48,56},{56,48},{64,72... | collective-permute-start | bytes 12976136 | tf_op jit(solution)/shard_map/ppermute | solution.py:105
  130.4 0.9 copy.32.qseg_ref
  131.3 0.6 fusion.29
  133.1 0.1 concatenate.20
  133.2 0.7 convolution_convert_fusion.1
  134.0 0.9 copy.31
  134.8 1.0 slice_reduce_fusion.7
  135.9 1.9 collective-permute-done.7.second_ref
  137.7 1.0 slice_reduce_fusion.5
  138.7 0.1 concatenate.24
  138.8 0.1 concatenate.23
  138.9 1.2 and_select_fusion.1
  140.1 0.6 concatenate.25.meta_ref
  140.7 106.8 %shard_map.55 = bf16[512,512]{1,0:T(8,128)(2,1)} custom-call(s32[81]{0:T(128)} %concatenate.25.meta_ref, bf16[512,512]{1,0:T(8,128)(2,1)} %bitcast.53, f32[512,1]{1,0:T(8,128)} %copy.32.qseg_ref, bf16[8,3,528,256]{3,2,1,0:T(8,128)(2,1)} %copy-done.1, bf16[8,2,528,256]{3,2,1,0:T(8,128)(2,1)} %collective-permute-done.7.second_ref), custom_call_target="tpu_custom_call" | custom-call | flops 21474836480 | bytes 11862016 | tf_op jit(solution)/shard_map/pallas_call | solution.py:228
  (10 shorter events, 0.1 us)
Async XLA Ops:
  0.0 55.7 %copy-start = (bf16[1024,512]{1,0:T(8,128)(2,1)S(1)}, bf16[1024,512]{1,0:T(8,128)(2,1)}, u32[]{:S(2)}) copy-start(bf16[1024,512]{1,0:T(8,128)(2,1)} %param.5) | copy-start | bytes 3145732
  4.9 12.1 %all-to-all-start = ((bf16[8,1,128,256]{3,2,1,0:T(8,128)(2,1)}), bf16[8,1,128,256]{3,2,1,0:T(8,128)(2,1)S(1)}, u32[]{:S(2)}, u32[]{:S(2)}) async-start(bf16[8,1,128,256]{3,2,1,0:T(8,128)(2,1)} %copy.25), calls=%async_computation | async-start | bytes 1048576 | tf_op jit(solution)/shard_map/all_to_all | solution.py:58
  17.6 11.9 %collective-permute-start.1 = (bf16[528,256]{1,0:T(8,128)(2,1)S(1)}, bf16[528,256]{1,0:T(8,128)(2,1)S(1)}, u32[]{:S(2)}, u32[]{:S(2)}) collective-permute-start(bf16[528,256]{1,0:T(8,128)(2,1)S(1)} %get-tuple-element.28), channel_id=1, source_target_pairs={{0,32},{8,40},{16,48},{24,56},{32,64},{40,72},{48,80},{56,88},{64,... | collective-permute-start | bytes 811016 | tf_op jit(solution)/shard_map/ppermute | solution.py:14
  21.5 12.8 %collective-permute-start = (bf16[528,256]{1,0:T(8,128)(2,1)S(1)}, bf16[528,256]{1,0:T(8,128)(2,1)S(1)}, u32[]{:S(2)}, u32[]{:S(2)}) collective-permute-start(bf16[528,256]{1,0:T(8,128)(2,1)S(1)} %get-tuple-element.28), channel_id=1, source_target_pairs={{0,16},{8,24},{16,32},{24,40},{32,48},{40,56},{48,64},{56,72},{64,... | collective-permute-start | bytes 811016 | tf_op jit(solution)/shard_map/ppermute | solution.py:14
  34.3 18.2 %copy-start.2 = (bf16[528,256]{1,0:T(8,128)(2,1)}, bf16[528,256]{1,0:T(8,128)(2,1)S(1)}, u32[]{:S(2)}) copy-start(bf16[528,256]{1,0:T(8,128)(2,1)S(1)} %collective-permute-done) | copy-start | bytes 811012
  34.4 18.1 %collective-permute-start.2 = (bf16[3,528,256]{2,1,0:T(8,128)(2,1)S(1)}, bf16[3,528,256]{2,1,0:T(8,128)(2,1)S(1)}, u32[]{:S(2)}, u32[]{:S(2)}) collective-permute-start(bf16[3,528,256]{2,1,0:T(8,128)(2,1)S(1)} %get-tuple-element.26), channel_id=1, source_target_pairs={{0,1},{1,0},{2,3},{3,2},{4,5},{5,4},{6,7},{7,6},{8,9},{9,8},{10,11... | collective-permute-start | bytes 2433032 | tf_op jit(solution)/shard_map/ppermute | solution.py:84
  53.8 34.8 %collective-permute-start.3 = (bf16[2,3,528,256]{3,2,1,0:T(8,128)(2,1)}, bf16[2,3,528,256]{3,2,1,0:T(8,128)(2,1)}, u32[]{:S(2)}, u32[]{:S(2)}) collective-permute-start(bf16[2,3,528,256]{3,2,1,0:T(8,128)(2,1)} %pad_maximum_fusion), channel_id=1, source_target_pairs={{0,2},{1,3},{2,4},{3,5},{4,6},{5,7},{6,0},{7,1},{8,10},{9,11},{10,... | collective-permute-start | bytes 4866056 | tf_op jit(solution)/shard_map/ppermute | solution.py:89
  55.7 35.7 %collective-permute-start.4 = (bf16[2,3,528,256]{3,2,1,0:T(8,128)(2,1)}, bf16[2,3,528,256]{3,2,1,0:T(8,128)(2,1)}, u32[]{:S(2)}, u32[]{:S(2)}) collective-permute-start(bf16[2,3,528,256]{3,2,1,0:T(8,128)(2,1)} %pad_maximum_fusion), channel_id=1, source_target_pairs={{0,6},{1,7},{2,0},{3,1},{4,2},{5,3},{6,4},{7,5},{8,14},{9,15},{10,... | collective-permute-start | bytes 4866056 | tf_op jit(solution)/shard_map/ppermute | solution.py:89
  57.8 43.2 %all-to-all-start.1 = ((bf16[8,1,128,512]{3,2,1,0:T(8,128)(2,1)}), bf16[8,1,128,512]{3,2,1,0:T(8,128)(2,1)S(1)}, u32[]{:S(2)}, u32[]{:S(2)}) async-start(bf16[8,1,128,512]{3,2,1,0:T(8,128)(2,1)} %copy.29), calls=%async_computation.1 | async-start | bytes 2097152 | tf_op jit(solution)/shard_map/all_to_all | solution.py:87
  101.0 14.6 %collective-permute-start.5 = (bf16[3,528,256]{2,1,0:T(8,128)(2,1)}, bf16[3,528,256]{2,1,0:T(8,128)(2,1)}, u32[]{:S(2)}, u32[]{:S(2)}) collective-permute-start(bf16[3,528,256]{2,1,0:T(8,128)(2,1)} %slice_bitcast_fusion.1), channel_id=1, source_target_pairs={{0,2},{1,3},{2,4},{3,5},{4,6},{5,7},{6,0},{7,1},{8,10},{9,11},{10,... | collective-permute-start | bytes 2433032 | tf_op jit(solution)/shard_map/ppermute | solution.py:89
  101.8 16.3 %collective-permute-start.6 = (bf16[3,528,256]{2,1,0:T(8,128)(2,1)}, bf16[3,528,256]{2,1,0:T(8,128)(2,1)S(1)}, u32[]{:S(2)}, u32[]{:S(2)}) collective-permute-start(bf16[3,528,256]{2,1,0:T(8,128)(2,1)} %slice_bitcast_fusion), channel_id=1, source_target_pairs={{0,6},{1,7},{2,0},{3,1},{4,2},{5,3},{6,4},{7,5},{8,14},{9,15},{10,... | collective-permute-start | bytes 2433032 | tf_op jit(solution)/shard_map/ppermute | solution.py:89
  119.7 2.7 %copy-start.1 = (bf16[8,3,528,256]{3,2,1,0:T(8,128)(2,1)}, bf16[8,3,528,256]{3,2,1,0:T(8,128)(2,1)S(1)}, u32[]{:S(2)}) copy-start(bf16[8,3,528,256]{3,2,1,0:T(8,128)(2,1)S(1)} %constant_dynamic-update-slice_fusion.first_ref) | copy-start | bytes 19464196
  124.8 12.9 %collective-permute-start.7 = (bf16[8,2,528,256]{3,2,1,0:T(8,128)(2,1)}, bf16[8,2,528,256]{3,2,1,0:T(8,128)(2,1)}, u32[]{:S(2)}, u32[]{:S(2)}) collective-permute-start(bf16[8,2,528,256]{3,2,1,0:T(8,128)(2,1)} %constant_dynamic-slice_fusion), channel_id=1, source_target_pairs={{0,8},{8,0},{16,24},{24,16},{32,40},{40,32},{48,56},{56,48},{64,72... | collective-permute-start | bytes 12976136 | tf_op jit(solution)/shard_map/ppermute | solution.py:105
